TPU v7x, 512 devices: a whole 4x8x8 slice. The times are simulated.
512 devices in a mesh: sep: 8 (over y), row: 8 (over z), col: 8 (over x, core).
Axes of the slice: x: 4, y: 8, z: 8, core: 2. Of those that a mesh axis runs over, the one named last changes fastest.
Arguments:
- right_sides: float32 [2, 16, 32768], P(None, None, ('sep', 'row', 'col')), may hold values from -6 to 6
- inverse_diag: float32 [8, 4096, 4096], P('sep', ('row', 'col')), may hold values from -0.09375 to 0.09375
- lower_blocks: float32 [8, 2048, 4096], P('sep', ('row', 'col')), may hold values from -0.09375 to 0.09375
- targets: int32 [8, 2048], P('sep', ('row', 'col')), may hold values from 0 to 32767, as said below
- counts: int32 [8, 64], P('sep', ('row', 'col')), may hold values from 0 to 32, as said below
Outputs:
- solution: float32 [2, 16, 32768], P(None, None, ('sep', 'row', 'col'))
Inputs may be any that keep to these rules, and one draw needn't show every extreme that they name: For every separator s and lower row j: targets[s, j] // 4096 > s, except for the last separator whose counts are all zero; and (targets[s, j] % 4096) // 64 == j // 32. The last separator's counts are zero; every other separator has a block with exactly 32 live rows, and the others at least one.
All inputs are finite; a program needn't handle non-finite values.
Results may differ from a plain program's by a relative error of at most 0.0001.
Values sent between devices are 32-bit elements; how exact they have to be, the bound alone decides.
No kernel may reach another device: no remote copies, remote signals or barrier semaphores. Data moves between devices by JAX's collectives and lax.ppermute only.
A program may use at most 64 MiB of HBM per device.

v0:
```python
import jax
import jax.numpy as jnp
from jax import lax
from jax.sharding import PartitionSpec as P

W = 4096


def passed_along(block, axis, distance):
    devices = range(lax.axis_size(axis))
    route = [(i - distance, i) for i in devices if i - distance in devices]
    return lax.ppermute(block, axis, route)


def shards(right_sides, inverse_diag, lower_blocks, targets, counts):
    levels = lax.axis_size("sep")
    own_level = lax.axis_index("sep")
    batches = right_sides.shape[0]
    width_rhs = right_sides.shape[1]
    own_rows = right_sides.shape[2]
    diag_rows = inverse_diag[0]
    lower_rows = lower_blocks[0]
    lower_count = lower_rows.shape[0]
    live = jnp.arange(lower_count, dtype=jnp.int32) < counts[0, 0]
    places = targets[0] // W * own_rows + targets[0] % own_rows

    def solve_piece(segment):
        return lax.dot_general(
            segment,
            diag_rows,
            (((1,), (1,)), ((), ())),
            precision=lax.Precision.HIGHEST,
            preferred_element_type=jnp.float32,
        )

    def lower_piece(segment):
        return lax.dot_general(
            segment,
            lower_rows,
            (((1,), (1,)), ((), ())),
            precision=lax.Precision.HIGHEST,
            preferred_element_type=jnp.float32,
        )

    def one_turn(turn, state):
        carried, solved_all = state
        batch_now = turn // levels
        active = turn % levels == own_level
        batch_now = jnp.clip(batch_now, 0, batches - 1)
        given = lax.dynamic_index_in_dim(right_sides, batch_now, 0, keepdims=False)
        resid = given - lax.dynamic_slice_in_dim(carried, own_level * own_rows, own_rows, 1)
        solved = solve_piece(lax.all_gather(resid, ("row", "col"), axis=1, tiled=True))
        update = lower_piece(lax.all_gather(solved, ("row", "col"), axis=1, tiled=True))
        update = jnp.where(live[None, :], update, jnp.float32(0.0))
        carried = carried.at[:, places].add(update)
        former = lax.dynamic_index_in_dim(solved_all, batch_now, 0, keepdims=False)
        solved_all = lax.dynamic_update_index_in_dim(
            solved_all, jnp.where(active, solved, former), batch_now, 0
        )
        carried = passed_along(carried, "sep", 1)
        return (carried, solved_all)

    turns = batches * levels
    start_carry = jnp.zeros((width_rhs, levels * own_rows), jnp.float32)
    start_solved = jnp.zeros(right_sides.shape, jnp.float32)
    final_carry, solution = lax.fori_loop(0, turns, one_turn, (start_carry, start_solved))
    return solution


def solution(mesh):
    placed = (
        P(None, None, ("sep", "row", "col")),
        P("sep", ("row", "col"), None),
        P("sep", ("row", "col"), None),
        P("sep", ("row", "col")),
        P("sep", ("row", "col")),
    )
    return jax.shard_map(
        shards,
        mesh=mesh,
        in_specs=placed,
        out_specs=P(None, None, ("sep", "row", "col")),
        check_vma=False,
    )
```

profile of v0, /device:TPU:32, one launch (start us, length us, event | category | flops | bytes accessed | tf_op | source)
XLA Modules:
  0.0 1837.8 jit_solution(4809233854240847362)
XLA Ops:
  1.4 1835.8 %while.18 = (s32[]{:T(128)}, f32[16,512]{0,1:T(8,128)S(1)}, f32[2,16,64]{2,1,0:T(8,128)S(1)}, s32[32]{0:T(128)S(1)}, f32[2,16,64]{2,1,0:T(8,128)S(1)}, /*index=5...) while((s32[]{:T(128)}, f32[16,512]{0,1:T(8,128)S(1)}, ...), condition=%wide.region_2.3_spmd.clone, body=%wide.region_0.2_spmd.clone.sunk | while | flops 75500688 | bytes 11338590 | solution.py:66
  1.6 56.5 %all-gather.6 = f32[64,64,16]{1,2,0:T(8,128)S(1)} all-gather(f32[1,64,16]{1,2,0:T(8,128)S(1)} %fusion.22), channel_id=1, replica_groups=mesh['sep'=8,'row'=8,'col'=8] {'row','col'}, dimensions={0}, use_global_device_ids=true | all-gather | bytes 266240 | tf_op jit(solution)/shard_map/while/body/eval_jaxpr/all_gather | solution.py:52
  60.2 49.5 %all-gather.7 = f32[64,64,16]{1,2,0:T(8,128)S(1)} all-gather(f32[1,64,16]{1,2,0:T(8,128)S(1)} %bitcast.71), channel_id=1, replica_groups=mesh['sep'=8,'row'=8,'col'=8] {'row','col'}, dimensions={0}, use_global_device_ids=true | all-gather | bytes 266240 | tf_op jit(solution)/shard_map/while/body/eval_jaxpr/all_gather | solution.py:53
  124.3 48.0 %all-gather.6 = f32[64,64,16]{1,2,0:T(8,128)S(1)} all-gather(f32[1,64,16]{1,2,0:T(8,128)S(1)} %fusion.22), channel_id=1, replica_groups=mesh['sep'=8,'row'=8,'col'=8] {'row','col'}, dimensions={0}, use_global_device_ids=true | all-gather | bytes 266240 | tf_op jit(solution)/shard_map/while/body/eval_jaxpr/all_gather | solution.py:52
  174.4 49.5 %all-gather.7 = f32[64,64,16]{1,2,0:T(8,128)S(1)} all-gather(f32[1,64,16]{1,2,0:T(8,128)S(1)} %bitcast.71), channel_id=1, replica_groups=mesh['sep'=8,'row'=8,'col'=8] {'row','col'}, dimensions={0}, use_global_device_ids=true | all-gather | bytes 266240 | tf_op jit(solution)/shard_map/while/body/eval_jaxpr/all_gather | solution.py:53
  238.5 48.0 %all-gather.6 = f32[64,64,16]{1,2,0:T(8,128)S(1)} all-gather(f32[1,64,16]{1,2,0:T(8,128)S(1)} %fusion.22), channel_id=1, replica_groups=mesh['sep'=8,'row'=8,'col'=8] {'row','col'}, dimensions={0}, use_global_device_ids=true | all-gather | bytes 266240 | tf_op jit(solution)/shard_map/while/body/eval_jaxpr/all_gather | solution.py:52
  288.6 49.5 %all-gather.7 = f32[64,64,16]{1,2,0:T(8,128)S(1)} all-gather(f32[1,64,16]{1,2,0:T(8,128)S(1)} %bitcast.71), channel_id=1, replica_groups=mesh['sep'=8,'row'=8,'col'=8] {'row','col'}, dimensions={0}, use_global_device_ids=true | all-gather | bytes 266240 | tf_op jit(solution)/shard_map/while/body/eval_jaxpr/all_gather | solution.py:53
  402.8 49.5 %all-gather.7 = f32[64,64,16]{1,2,0:T(8,128)S(1)} all-gather(f32[1,64,16]{1,2,0:T(8,128)S(1)} %bitcast.71), channel_id=1, replica_groups=mesh['sep'=8,'row'=8,'col'=8] {'row','col'}, dimensions={0}, use_global_device_ids=true | all-gather | bytes 266240 | tf_op jit(solution)/shard_map/while/body/eval_jaxpr/all_gather | solution.py:53
  517.0 49.5 %all-gather.7 = f32[64,64,16]{1,2,0:T(8,128)S(1)} all-gather(f32[1,64,16]{1,2,0:T(8,128)S(1)} %bitcast.71), channel_id=1, replica_groups=mesh['sep'=8,'row'=8,'col'=8] {'row','col'}, dimensions={0}, use_global_device_ids=true | all-gather | bytes 266240 | tf_op jit(solution)/shard_map/while/body/eval_jaxpr/all_gather | solution.py:53
  631.3 49.5 %all-gather.7 = f32[64,64,16]{1,2,0:T(8,128)S(1)} all-gather(f32[1,64,16]{1,2,0:T(8,128)S(1)} %bitcast.71), channel_id=1, replica_groups=mesh['sep'=8,'row'=8,'col'=8] {'row','col'}, dimensions={0}, use_global_device_ids=true | all-gather | bytes 266240 | tf_op jit(solution)/shard_map/while/body/eval_jaxpr/all_gather | solution.py:53
  745.5 49.5 %all-gather.7 = f32[64,64,16]{1,2,0:T(8,128)S(1)} all-gather(f32[1,64,16]{1,2,0:T(8,128)S(1)} %bitcast.71), channel_id=1, replica_groups=mesh['sep'=8,'row'=8,'col'=8] {'row','col'}, dimensions={0}, use_global_device_ids=true | all-gather | bytes 266240 | tf_op jit(solution)/shard_map/while/body/eval_jaxpr/all_gather | solution.py:53
  859.7 49.5 %all-gather.7 = f32[64,64,16]{1,2,0:T(8,128)S(1)} all-gather(f32[1,64,16]{1,2,0:T(8,128)S(1)} %bitcast.71), channel_id=1, replica_groups=mesh['sep'=8,'row'=8,'col'=8] {'row','col'}, dimensions={0}, use_global_device_ids=true | all-gather | bytes 266240 | tf_op jit(solution)/shard_map/while/body/eval_jaxpr/all_gather | solution.py:53
  973.9 49.5 %all-gather.7 = f32[64,64,16]{1,2,0:T(8,128)S(1)} all-gather(f32[1,64,16]{1,2,0:T(8,128)S(1)} %bitcast.71), channel_id=1, replica_groups=mesh['sep'=8,'row'=8,'col'=8] {'row','col'}, dimensions={0}, use_global_device_ids=true | all-gather | bytes 266240 | tf_op jit(solution)/shard_map/while/body/eval_jaxpr/all_gather | solution.py:53
  1088.1 49.5 %all-gather.7 = f32[64,64,16]{1,2,0:T(8,128)S(1)} all-gather(f32[1,64,16]{1,2,0:T(8,128)S(1)} %bitcast.71), channel_id=1, replica_groups=mesh['sep'=8,'row'=8,'col'=8] {'row','col'}, dimensions={0}, use_global_device_ids=true | all-gather | bytes 266240 | tf_op jit(solution)/shard_map/while/body/eval_jaxpr/all_gather | solution.py:53
  1152.2 48.0 %all-gather.6 = f32[64,64,16]{1,2,0:T(8,128)S(1)} all-gather(f32[1,64,16]{1,2,0:T(8,128)S(1)} %fusion.22), channel_id=1, replica_groups=mesh['sep'=8,'row'=8,'col'=8] {'row','col'}, dimensions={0}, use_global_device_ids=true | all-gather | bytes 266240 | tf_op jit(solution)/shard_map/while/body/eval_jaxpr/all_gather | solution.py:52
  1202.3 49.5 %all-gather.7 = f32[64,64,16]{1,2,0:T(8,128)S(1)} all-gather(f32[1,64,16]{1,2,0:T(8,128)S(1)} %bitcast.71), channel_id=1, replica_groups=mesh['sep'=8,'row'=8,'col'=8] {'row','col'}, dimensions={0}, use_global_device_ids=true | all-gather | bytes 266240 | tf_op jit(solution)/shard_map/while/body/eval_jaxpr/all_gather | solution.py:53
  1266.4 48.0 %all-gather.6 = f32[64,64,16]{1,2,0:T(8,128)S(1)} all-gather(f32[1,64,16]{1,2,0:T(8,128)S(1)} %fusion.22), channel_id=1, replica_groups=mesh['sep'=8,'row'=8,'col'=8] {'row','col'}, dimensions={0}, use_global_device_ids=true | all-gather | bytes 266240 | tf_op jit(solution)/shard_map/while/body/eval_jaxpr/all_gather | solution.py:52
  1316.5 49.5 %all-gather.7 = f32[64,64,16]{1,2,0:T(8,128)S(1)} all-gather(f32[1,64,16]{1,2,0:T(8,128)S(1)} %bitcast.71), channel_id=1, replica_groups=mesh['sep'=8,'row'=8,'col'=8] {'row','col'}, dimensions={0}, use_global_device_ids=true | all-gather | bytes 266240 | tf_op jit(solution)/shard_map/while/body/eval_jaxpr/all_gather | solution.py:53
  1380.6 48.0 %all-gather.6 = f32[64,64,16]{1,2,0:T(8,128)S(1)} all-gather(f32[1,64,16]{1,2,0:T(8,128)S(1)} %fusion.22), channel_id=1, replica_groups=mesh['sep'=8,'row'=8,'col'=8] {'row','col'}, dimensions={0}, use_global_device_ids=true | all-gather | bytes 266240 | tf_op jit(solution)/shard_map/while/body/eval_jaxpr/all_gather | solution.py:52
  1430.7 49.5 %all-gather.7 = f32[64,64,16]{1,2,0:T(8,128)S(1)} all-gather(f32[1,64,16]{1,2,0:T(8,128)S(1)} %bitcast.71), channel_id=1, replica_groups=mesh['sep'=8,'row'=8,'col'=8] {'row','col'}, dimensions={0}, use_global_device_ids=true | all-gather | bytes 266240 | tf_op jit(solution)/shard_map/while/body/eval_jaxpr/all_gather | solution.py:53
  1544.9 49.5 %all-gather.7 = f32[64,64,16]{1,2,0:T(8,128)S(1)} all-gather(f32[1,64,16]{1,2,0:T(8,128)S(1)} %bitcast.71), channel_id=1, replica_groups=mesh['sep'=8,'row'=8,'col'=8] {'row','col'}, dimensions={0}, use_global_device_ids=true | all-gather | bytes 266240 | tf_op jit(solution)/shard_map/while/body/eval_jaxpr/all_gather | solution.py:53
  1609.0 48.0 %all-gather.6 = f32[64,64,16]{1,2,0:T(8,128)S(1)} all-gather(f32[1,64,16]{1,2,0:T(8,128)S(1)} %fusion.22), channel_id=1, replica_groups=mesh['sep'=8,'row'=8,'col'=8] {'row','col'}, dimensions={0}, use_global_device_ids=true | all-gather | bytes 266240 | tf_op jit(solution)/shard_map/while/body/eval_jaxpr/all_gather | solution.py:52
  1659.1 49.5 %all-gather.7 = f32[64,64,16]{1,2,0:T(8,128)S(1)} all-gather(f32[1,64,16]{1,2,0:T(8,128)S(1)} %bitcast.71), channel_id=1, replica_groups=mesh['sep'=8,'row'=8,'col'=8] {'row','col'}, dimensions={0}, use_global_device_ids=true | all-gather | bytes 266240 | tf_op jit(solution)/shard_map/while/body/eval_jaxpr/all_gather | solution.py:53
  1773.3 49.5 %all-gather.7 = f32[64,64,16]{1,2,0:T(8,128)S(1)} all-gather(f32[1,64,16]{1,2,0:T(8,128)S(1)} %bitcast.71), channel_id=1, replica_groups=mesh['sep'=8,'row'=8,'col'=8] {'row','col'}, dimensions={0}, use_global_device_ids=true | all-gather | bytes 266240 | tf_op jit(solution)/shard_map/while/body/eval_jaxpr/all_gather | solution.py:53
  (338 shorter events, 699.8 us)
Async XLA Ops:
  58.1 1.2 copy-start
  112.5 11.7 collective-permute-start
  226.7 11.7 collective-permute-start
  286.5 1.2 copy-start
  340.9 11.7 collective-permute-start
  400.7 1.2 copy-start
  455.1 11.7 collective-permute-start
  514.9 1.2 copy-start
  569.3 11.7 collective-permute-start
  629.1 1.2 copy-start
  683.5 11.7 collective-permute-start
  797.7 11.7 collective-permute-start
  857.5 1.2 copy-start
  911.9 11.7 collective-permute-start
  971.7 1.2 copy-start
  1026.1 11.7 collective-permute-start
  1085.9 1.2 copy-start
  1140.3 11.7 collective-permute-start
  1254.5 11.7 collective-permute-start
  1368.7 11.7 collective-permute-start
  1482.9 11.7 collective-permute-start
  1597.1 11.7 collective-permute-start
  1711.3 11.7 collective-permute-start
  1825.5 11.7 collective-permute-start
  (27 other events, 28.5 us)
where the time goes:
time: 1840 us
  blocking collectives  1570 us (85%)
  waiting for transfers between devices  155 us (8%)
  local copies, waits for them, and re-layouts  33.2 us (2%)
  starting transfers between devices  31.4 us (2%)
  other arithmetic  25.5 us (1%)
  matrix products  23 us (1%)
    all_gather x16, blocking collectives, one_turn(): lax.all_gather(solved, ('row', 'col'), axis=1, tiled=True)  792 us
    all_gather x16, blocking collectives, one_turn(): lax.all_gather(resid, ('row', 'col'), axis=1, tiled=True)  776 us
    ppermute x16, waiting for transfers between devices, passed_along(): return lax.ppermute(block, axis, route)  155 us
  transfers between devices with their start and end apart: 16, of which 16 were waited for; matrix products, arithmetic and copies ran while one was open for 0% of the time, Pallas kernels for 0%

commit v1 on v0

--- a/solution.py
+++ b/solution.py
@@ -4,6 +4,11 @@
 from jax.sharding import PartitionSpec as P
 
 W = 4096
+
+
+def tiled_gather(x, axis, dim):
+    copies = jnp.concatenate([x] * lax.axis_size(axis), axis=dim)
+    return lax.all_to_all(copies, axis, dim, dim, tiled=True)
 
 
 def passed_along(block, axis, distance):
@@ -49,7 +54,7 @@
         batch_now = jnp.clip(batch_now, 0, batches - 1)
         given = lax.dynamic_index_in_dim(right_sides, batch_now, 0, keepdims=False)
         resid = given - lax.dynamic_slice_in_dim(carried, own_level * own_rows, own_rows, 1)
-        solved = solve_piece(lax.all_gather(resid, ("row", "col"), axis=1, tiled=True))
+        solved = solve_piece(tiled_gather(resid, ("row", "col"), 1))
         update = lower_piece(lax.all_gather(solved, ("row", "col"), axis=1, tiled=True))
         update = jnp.where(live[None, :], update, jnp.float32(0.0))
         carried = carried.at[:, places].add(update)

time: 1840 us -> 1430 us (0.78)
  blocking collectives: 1570 us -> 783 us
  waiting for transfers between devices: 155 us -> 350 us
  starting transfers between devices: 31.4 us -> 137 us
  local copies, waits for them, and re-layouts: 33.2 us -> 81.8 us
  other arithmetic: 25.5 us -> 45.2 us
    all_gather x16 -> x0, blocking collectives: 776 us -> none  [one_turn(): lax.all_gather(resid, ('row', 'col'), axis=1, tiled=True)]
    all_to_all x0 -> x16, waiting for transfers between devices: none -> 195 us  [tiled_gather(): return lax.all_to_all(copies, axis, dim, dim, tiled=True)]
    all_to_all x0 -> x16, starting transfers between devices: none -> 105 us  [tiled_gather(): return lax.all_to_all(copies, axis, dim, dim, tiled=True)]
    while x128 -> x144, local copies, waits for them, and re-layouts: 24.4 us -> 50.5 us
    all_to_all x0 -> x80, local copies, waits for them, and re-layouts: none -> 22.4 us  [tiled_gather(): return lax.all_to_all(copies, axis, dim, dim, tiled=True)]
    all_to_all x0 -> x16, other arithmetic: none -> 19.7 us  [tiled_gather(): return lax.all_to_all(copies, axis, dim, dim, tiled=True)]
  transfers between devices with their start and end apart: 16 -> 32, of which waited for: 16 -> 32; matrix products, arithmetic and copies ran while one was open for 0% -> 1% of each run, Pallas kernels for 0% -> 0%
where the time goes in v1:
time: 1430 us; the launch traced here: 1420 us
  blocking collectives  783 us (55%)
  waiting for transfers between devices  350 us (24%)
  starting transfers between devices  137 us (10%)
  local copies, waits for them, and re-layouts  81.8 us (6%)
  other arithmetic  45.2 us (3%)
  matrix products  23 us (2%)
    all_gather x16, blocking collectives, one_turn(): lax.all_gather(solved, ('row', 'col'), axis=1, tiled=True)  783 us
    all_to_all x16, waiting for transfers between devices, tiled_gather(): return lax.all_to_all(copies, axis, dim, dim, tiled=True)  195 us
    ppermute x16, waiting for transfers between devices, passed_along(): return lax.ppermute(block, axis, route)  155 us
    all_to_all x16, starting transfers between devices, tiled_gather(): return lax.all_to_all(copies, axis, dim, dim, tiled=True)  105 us
    while x144, local copies, waits for them, and re-layouts  50.5 us
    ppermute x16, starting transfers between devices, passed_along(): return lax.ppermute(block, axis, route)  31.4 us
  transfers between devices with their start and end apart: 32, of which 32 were waited for; matrix products, arithmetic and copies ran while one was open for 1% of the time, Pallas kernels for 0%

profile of v1, /device:TPU:32, one launch (start us, length us, event | category | flops | bytes accessed | tf_op | source)
XLA Modules:
  0.0 1422.3 jit_solution(3346094493391141695)
XLA Ops:
  1.4 1420.2 %while.18 = (s32[]{:T(128)}, f32[16,512]{0,1:T(8,128)S(1)}, f32[2,16,64]{2,1,0:T(8,128)S(1)}, s32[32]{0:T(128)S(1)}, f32[2,16,64]{2,1,0:T(8,128)S(1)}, /*index=5...) while((s32[]{:T(128)}, f32[16,512]{0,1:T(8,128)S(1)}, ...), condition=%wide.region_2.3_spmd.clone, body=%wide.region_0.2_spmd.clone.sunk | while | flops 75500688 | bytes 15004562 | solution.py:71
  3.3 13.8 all-to-all-start
  17.8 12.2 all-to-all-done
  34.0 48.9 %all-gather.3 = f32[64,64,16]{1,2,0:T(8,128)S(1)} all-gather(f32[1,64,16]{1,2,0:T(8,128)S(1)} %bitcast.71), channel_id=1, replica_groups=mesh['sep'=8,'row'=8,'col'=8] {'row','col'}, dimensions={0}, use_global_device_ids=true | all-gather | bytes 266240 | tf_op jit(solution)/shard_map/while/body/eval_jaxpr/all_gather | solution.py:58
  106.1 12.2 all-to-all-done
  122.3 48.9 %all-gather.3 = f32[64,64,16]{1,2,0:T(8,128)S(1)} all-gather(f32[1,64,16]{1,2,0:T(8,128)S(1)} %bitcast.71), channel_id=1, replica_groups=mesh['sep'=8,'row'=8,'col'=8] {'row','col'}, dimensions={0}, use_global_device_ids=true | all-gather | bytes 266240 | tf_op jit(solution)/shard_map/while/body/eval_jaxpr/all_gather | solution.py:58
  194.4 12.2 all-to-all-done
  210.6 48.9 %all-gather.3 = f32[64,64,16]{1,2,0:T(8,128)S(1)} all-gather(f32[1,64,16]{1,2,0:T(8,128)S(1)} %bitcast.71), channel_id=1, replica_groups=mesh['sep'=8,'row'=8,'col'=8] {'row','col'}, dimensions={0}, use_global_device_ids=true | all-gather | bytes 266240 | tf_op jit(solution)/shard_map/while/body/eval_jaxpr/all_gather | solution.py:58
  298.9 48.9 %all-gather.3 = f32[64,64,16]{1,2,0:T(8,128)S(1)} all-gather(f32[1,64,16]{1,2,0:T(8,128)S(1)} %bitcast.71), channel_id=1, replica_groups=mesh['sep'=8,'row'=8,'col'=8] {'row','col'}, dimensions={0}, use_global_device_ids=true | all-gather | bytes 266240 | tf_op jit(solution)/shard_map/while/body/eval_jaxpr/all_gather | solution.py:58
  387.2 48.9 %all-gather.3 = f32[64,64,16]{1,2,0:T(8,128)S(1)} all-gather(f32[1,64,16]{1,2,0:T(8,128)S(1)} %bitcast.71), channel_id=1, replica_groups=mesh['sep'=8,'row'=8,'col'=8] {'row','col'}, dimensions={0}, use_global_device_ids=true | all-gather | bytes 266240 | tf_op jit(solution)/shard_map/while/body/eval_jaxpr/all_gather | solution.py:58
  475.5 48.9 %all-gather.3 = f32[64,64,16]{1,2,0:T(8,128)S(1)} all-gather(f32[1,64,16]{1,2,0:T(8,128)S(1)} %bitcast.71), channel_id=1, replica_groups=mesh['sep'=8,'row'=8,'col'=8] {'row','col'}, dimensions={0}, use_global_device_ids=true | all-gather | bytes 266240 | tf_op jit(solution)/shard_map/while/body/eval_jaxpr/all_gather | solution.py:58
  563.8 48.9 %all-gather.3 = f32[64,64,16]{1,2,0:T(8,128)S(1)} all-gather(f32[1,64,16]{1,2,0:T(8,128)S(1)} %bitcast.71), channel_id=1, replica_groups=mesh['sep'=8,'row'=8,'col'=8] {'row','col'}, dimensions={0}, use_global_device_ids=true | all-gather | bytes 266240 | tf_op jit(solution)/shard_map/while/body/eval_jaxpr/all_gather | solution.py:58
  635.8 12.2 all-to-all-done
  652.0 48.9 %all-gather.3 = f32[64,64,16]{1,2,0:T(8,128)S(1)} all-gather(f32[1,64,16]{1,2,0:T(8,128)S(1)} %bitcast.71), channel_id=1, replica_groups=mesh['sep'=8,'row'=8,'col'=8] {'row','col'}, dimensions={0}, use_global_device_ids=true | all-gather | bytes 266240 | tf_op jit(solution)/shard_map/while/body/eval_jaxpr/all_gather | solution.py:58
  740.3 48.9 %all-gather.3 = f32[64,64,16]{1,2,0:T(8,128)S(1)} all-gather(f32[1,64,16]{1,2,0:T(8,128)S(1)} %bitcast.71), channel_id=1, replica_groups=mesh['sep'=8,'row'=8,'col'=8] {'row','col'}, dimensions={0}, use_global_device_ids=true | all-gather | bytes 266240 | tf_op jit(solution)/shard_map/while/body/eval_jaxpr/all_gather | solution.py:58
  828.6 48.9 %all-gather.3 = f32[64,64,16]{1,2,0:T(8,128)S(1)} all-gather(f32[1,64,16]{1,2,0:T(8,128)S(1)} %bitcast.71), channel_id=1, replica_groups=mesh['sep'=8,'row'=8,'col'=8] {'row','col'}, dimensions={0}, use_global_device_ids=true | all-gather | bytes 266240 | tf_op jit(solution)/shard_map/while/body/eval_jaxpr/all_gather | solution.py:58
  916.9 48.9 %all-gather.3 = f32[64,64,16]{1,2,0:T(8,128)S(1)} all-gather(f32[1,64,16]{1,2,0:T(8,128)S(1)} %bitcast.71), channel_id=1, replica_groups=mesh['sep'=8,'row'=8,'col'=8] {'row','col'}, dimensions={0}, use_global_device_ids=true | all-gather | bytes 266240 | tf_op jit(solution)/shard_map/while/body/eval_jaxpr/all_gather | solution.py:58
  989.0 12.2 all-to-all-done
  1005.2 48.9 %all-gather.3 = f32[64,64,16]{1,2,0:T(8,128)S(1)} all-gather(f32[1,64,16]{1,2,0:T(8,128)S(1)} %bitcast.71), channel_id=1, replica_groups=mesh['sep'=8,'row'=8,'col'=8] {'row','col'}, dimensions={0}, use_global_device_ids=true | all-gather | bytes 266240 | tf_op jit(solution)/shard_map/while/body/eval_jaxpr/all_gather | solution.py:58
  1077.2 12.2 all-to-all-done
  1093.5 48.9 %all-gather.3 = f32[64,64,16]{1,2,0:T(8,128)S(1)} all-gather(f32[1,64,16]{1,2,0:T(8,128)S(1)} %bitcast.71), channel_id=1, replica_groups=mesh['sep'=8,'row'=8,'col'=8] {'row','col'}, dimensions={0}, use_global_device_ids=true | all-gather | bytes 266240 | tf_op jit(solution)/shard_map/while/body/eval_jaxpr/all_gather | solution.py:58
  1181.8 48.9 %all-gather.3 = f32[64,64,16]{1,2,0:T(8,128)S(1)} all-gather(f32[1,64,16]{1,2,0:T(8,128)S(1)} %bitcast.71), channel_id=1, replica_groups=mesh['sep'=8,'row'=8,'col'=8] {'row','col'}, dimensions={0}, use_global_device_ids=true | all-gather | bytes 266240 | tf_op jit(solution)/shard_map/while/body/eval_jaxpr/all_gather | solution.py:58
  1270.1 48.9 %all-gather.3 = f32[64,64,16]{1,2,0:T(8,128)S(1)} all-gather(f32[1,64,16]{1,2,0:T(8,128)S(1)} %bitcast.71), channel_id=1, replica_groups=mesh['sep'=8,'row'=8,'col'=8] {'row','col'}, dimensions={0}, use_global_device_ids=true | all-gather | bytes 266240 | tf_op jit(solution)/shard_map/while/body/eval_jaxpr/all_gather | solution.py:58
  1358.3 48.9 %all-gather.3 = f32[64,64,16]{1,2,0:T(8,128)S(1)} all-gather(f32[1,64,16]{1,2,0:T(8,128)S(1)} %bitcast.71), channel_id=1, replica_groups=mesh['sep'=8,'row'=8,'col'=8] {'row','col'}, dimensions={0}, use_global_device_ids=true | all-gather | bytes 266240 | tf_op jit(solution)/shard_map/while/body/eval_jaxpr/all_gather | solution.py:58
  (466 shorter events, 550.0 us)
Async XLA Ops:
  3.3 26.7 %all-to-all-start = ((f32[64,1,1024]{2,1,0:T(1,128)}), f32[64,1,1024]{2,1,0:T(1,128)S(1)}, u32[]{:S(2)}, u32[]{:S(2)}) async-start(f32[64,1,1024]{2,1,0:T(1,128)} %reshape.58), calls=%async_computation | async-start | bytes 524288 | tf_op jit(solution)/shard_map/while/body/eval_jaxpr/all_to_all | solution.py:11
  85.7 11.7 collective-permute-start
  99.3 19.0 %all-to-all-start = ((f32[64,1,1024]{2,1,0:T(1,128)}), f32[64,1,1024]{2,1,0:T(1,128)S(1)}, u32[]{:S(2)}, u32[]{:S(2)}) async-start(f32[64,1,1024]{2,1,0:T(1,128)} %reshape.58), calls=%async_computation | async-start | bytes 524288 | tf_op jit(solution)/shard_map/while/body/eval_jaxpr/all_to_all | solution.py:11
  187.6 19.0 %all-to-all-start = ((f32[64,1,1024]{2,1,0:T(1,128)}), f32[64,1,1024]{2,1,0:T(1,128)S(1)}, u32[]{:S(2)}, u32[]{:S(2)}) async-start(f32[64,1,1024]{2,1,0:T(1,128)} %reshape.58), calls=%async_computation | async-start | bytes 524288 | tf_op jit(solution)/shard_map/while/body/eval_jaxpr/all_to_all | solution.py:11
  262.2 11.7 collective-permute-start
  275.9 19.0 %all-to-all-start = ((f32[64,1,1024]{2,1,0:T(1,128)}), f32[64,1,1024]{2,1,0:T(1,128)S(1)}, u32[]{:S(2)}, u32[]{:S(2)}) async-start(f32[64,1,1024]{2,1,0:T(1,128)} %reshape.58), calls=%async_computation | async-start | bytes 524288 | tf_op jit(solution)/shard_map/while/body/eval_jaxpr/all_to_all | solution.py:11
  350.5 11.7 collective-permute-start
  364.1 19.0 %all-to-all-start = ((f32[64,1,1024]{2,1,0:T(1,128)}), f32[64,1,1024]{2,1,0:T(1,128)S(1)}, u32[]{:S(2)}, u32[]{:S(2)}) async-start(f32[64,1,1024]{2,1,0:T(1,128)} %reshape.58), calls=%async_computation | async-start | bytes 524288 | tf_op jit(solution)/shard_map/while/body/eval_jaxpr/all_to_all | solution.py:11
  452.4 19.0 %all-to-all-start = ((f32[64,1,1024]{2,1,0:T(1,128)}), f32[64,1,1024]{2,1,0:T(1,128)S(1)}, u32[]{:S(2)}, u32[]{:S(2)}) async-start(f32[64,1,1024]{2,1,0:T(1,128)} %reshape.58), calls=%async_computation | async-start | bytes 524288 | tf_op jit(solution)/shard_map/while/body/eval_jaxpr/all_to_all | solution.py:11
  540.7 19.0 %all-to-all-start = ((f32[64,1,1024]{2,1,0:T(1,128)}), f32[64,1,1024]{2,1,0:T(1,128)S(1)}, u32[]{:S(2)}, u32[]{:S(2)}) async-start(f32[64,1,1024]{2,1,0:T(1,128)} %reshape.58), calls=%async_computation | async-start | bytes 524288 | tf_op jit(solution)/shard_map/while/body/eval_jaxpr/all_to_all | solution.py:11
  629.0 19.0 %all-to-all-start = ((f32[64,1,1024]{2,1,0:T(1,128)}), f32[64,1,1024]{2,1,0:T(1,128)S(1)}, u32[]{:S(2)}, u32[]{:S(2)}) async-start(f32[64,1,1024]{2,1,0:T(1,128)} %reshape.58), calls=%async_computation | async-start | bytes 524288 | tf_op jit(solution)/shard_map/while/body/eval_jaxpr/all_to_all | solution.py:11
  703.7 11.7 collective-permute-start
  717.3 19.0 %all-to-all-start = ((f32[64,1,1024]{2,1,0:T(1,128)}), f32[64,1,1024]{2,1,0:T(1,128)S(1)}, u32[]{:S(2)}, u32[]{:S(2)}) async-start(f32[64,1,1024]{2,1,0:T(1,128)} %reshape.58), calls=%async_computation | async-start | bytes 524288 | tf_op jit(solution)/shard_map/while/body/eval_jaxpr/all_to_all | solution.py:11
  792.0 11.7 collective-permute-start
  805.6 19.0 %all-to-all-start = ((f32[64,1,1024]{2,1,0:T(1,128)}), f32[64,1,1024]{2,1,0:T(1,128)S(1)}, u32[]{:S(2)}, u32[]{:S(2)}) async-start(f32[64,1,1024]{2,1,0:T(1,128)} %reshape.58), calls=%async_computation | async-start | bytes 524288 | tf_op jit(solution)/shard_map/while/body/eval_jaxpr/all_to_all | solution.py:11
  893.9 19.0 %all-to-all-start = ((f32[64,1,1024]{2,1,0:T(1,128)}), f32[64,1,1024]{2,1,0:T(1,128)S(1)}, u32[]{:S(2)}, u32[]{:S(2)}) async-start(f32[64,1,1024]{2,1,0:T(1,128)} %reshape.58), calls=%async_computation | async-start | bytes 524288 | tf_op jit(solution)/shard_map/while/body/eval_jaxpr/all_to_all | solution.py:11
  982.1 19.0 %all-to-all-start = ((f32[64,1,1024]{2,1,0:T(1,128)}), f32[64,1,1024]{2,1,0:T(1,128)S(1)}, u32[]{:S(2)}, u32[]{:S(2)}) async-start(f32[64,1,1024]{2,1,0:T(1,128)} %reshape.58), calls=%async_computation | async-start | bytes 524288 | tf_op jit(solution)/shard_map/while/body/eval_jaxpr/all_to_all | solution.py:11
  1056.8 11.7 collective-permute-start
  1070.4 19.0 %all-to-all-start = ((f32[64,1,1024]{2,1,0:T(1,128)}), f32[64,1,1024]{2,1,0:T(1,128)S(1)}, u32[]{:S(2)}, u32[]{:S(2)}) async-start(f32[64,1,1024]{2,1,0:T(1,128)} %reshape.58), calls=%async_computation | async-start | bytes 524288 | tf_op jit(solution)/shard_map/while/body/eval_jaxpr/all_to_all | solution.py:11
  1145.1 11.7 collective-permute-start
  1158.7 19.0 %all-to-all-start = ((f32[64,1,1024]{2,1,0:T(1,128)}), f32[64,1,1024]{2,1,0:T(1,128)S(1)}, u32[]{:S(2)}, u32[]{:S(2)}) async-start(f32[64,1,1024]{2,1,0:T(1,128)} %reshape.58), calls=%async_computation | async-start | bytes 524288 | tf_op jit(solution)/shard_map/while/body/eval_jaxpr/all_to_all | solution.py:11
  1233.4 11.7 collective-permute-start
  1247.0 19.0 %all-to-all-start = ((f32[64,1,1024]{2,1,0:T(1,128)}), f32[64,1,1024]{2,1,0:T(1,128)S(1)}, u32[]{:S(2)}, u32[]{:S(2)}) async-start(f32[64,1,1024]{2,1,0:T(1,128)} %reshape.58), calls=%async_computation | async-start | bytes 524288 | tf_op jit(solution)/shard_map/while/body/eval_jaxpr/all_to_all | solution.py:11
  1335.3 19.0 %all-to-all-start = ((f32[64,1,1024]{2,1,0:T(1,128)}), f32[64,1,1024]{2,1,0:T(1,128)S(1)}, u32[]{:S(2)}, u32[]{:S(2)}) async-start(f32[64,1,1024]{2,1,0:T(1,128)} %reshape.58), calls=%async_computation | async-start | bytes 524288 | tf_op jit(solution)/shard_map/while/body/eval_jaxpr/all_to_all | solution.py:11
  (43 other events, 131.7 us)
